TPU v7x, 256 devices: a whole 4x4x8 slice. The times are simulated.
256 devices in a mesh: row: 32 (over x, z), col: 8 (over y, core).
Axes of the slice: x: 4, y: 4, z: 8, core: 2. Of those that a mesh axis runs over, the one named last changes fastest.
Arguments:
- points: float32 [16384, 256], P('row'), may hold values from -6 to 6
- nugget: float32 [16384], P('row'), may hold values from 0.5 to 2
- weights: float32 [256], replicated, may hold values from 0.0005 to 0.005
- band_start: int32 [32], replicated, may hold values from 0 to 30, as said below
Outputs:
- factored: float32 [32, 4, 8, 512, 512], P('row', None, 'col')
Inputs may be any that keep to these rules, and one draw needn't show every extreme that they name: band_start[i] <= i - 1 for every i >= 1, band_start[0] = 0; band_start[17] = 0; the last tile row has band_start = 30.
All inputs are finite; a program needn't handle non-finite values.
Results may differ from a plain program's by a relative error of at most 0.0003.
Values sent between devices are 32-bit elements; how exact they have to be, the bound alone decides.
No kernel may reach another device: no remote copies, remote signals or barrier semaphores. Data moves between devices by JAX's collectives and lax.ppermute only.
A program may use at most 128 MiB of HBM per device.

v0:
```python
import jax
import jax.numpy as jnp
from jax import lax
from jax.sharding import PartitionSpec as P

HI = lax.Precision.HIGHEST


def mm(a, b):
    return lax.dot_general(
        a, b, (((1,), (1,)), ((), ())), precision=HI, preferred_element_type=jnp.float32
    )


def kernel_tile(xrow, xcol, weights):
    weighted = xrow * weights
    sq_row = jnp.sum(weighted * xrow, axis=1)
    sq_col = jnp.sum(xcol * xcol * weights, axis=1)
    cross = mm(weighted, xcol)
    dist_sq = jnp.maximum(sq_row[:, None] + sq_col[None, :] - 2.0 * cross, 0.0)
    dist = jnp.sqrt(3.0 * dist_sq)
    return (1.0 + dist) * jnp.exp(-dist)


def chol_inv(a):
    low = jnp.linalg.cholesky(a)
    eye = jnp.eye(a.shape[0], dtype=a.dtype)
    inv = jax.scipy.linalg.solve_triangular(low, eye, lower=True)
    return (low, inv)


def body(points, nugget, weights, band_start):
    n_row = lax.axis_size("row")
    n_col = lax.axis_size("col")
    blocks = n_row // n_col
    tile = points.shape[0]
    piece = tile // n_row
    my_row = lax.axis_index("row")
    my_col = lax.axis_index("col")
    chunks = points.reshape(n_row, piece, points.shape[1])
    recv = lax.all_to_all(chunks, "row", 0, 0, tiled=True)
    mine = lax.dynamic_slice_in_dim(
        recv.reshape(blocks, n_col, piece, points.shape[1]), my_col, 1, axis=1
    )[:, 0]
    sel = jnp.concatenate([recv[:2], mine], axis=0)
    tiles_x = lax.all_gather(sel, "row", axis=1, tiled=True)
    nug = lax.all_gather(nugget, "row", tiled=True)
    x0, x1 = (tiles_x[0], tiles_x[1])
    xcols = tiles_x[2:]
    n0, n1 = (nug[:tile], nug[tile : 2 * tile])
    cols = my_col + n_col * jnp.arange(blocks, dtype=jnp.int32)
    rows = jnp.concatenate([my_row[None], cols])
    xr_all = jnp.concatenate([points[None], xcols], axis=0).reshape(-1, points.shape[1])
    nr = len(rows)
    eye = jnp.eye(tile, dtype=jnp.float32)
    x01 = jnp.concatenate([x0, x1], axis=0)
    k01 = kernel_tile(x01, x01, weights)
    a00 = k01[:tile, :tile] + eye * n0[None, :]
    a10 = k01[tile:, :tile]
    a11 = k01[tile:, tile:] + eye * n1[None, :]
    kr = kernel_tile(xr_all, x01, weights).reshape(nr, tile, 2, tile)
    bs = band_start[rows]
    keep0 = (bs <= 0)[:, None, None]
    keep1 = ((bs <= 1) & (rows >= 1))[:, None, None]
    ar0 = jnp.where(keep0, kr[:, :, 0], 0.0)
    ar0 = ar0 + jnp.where((rows == 0)[:, None, None], eye * n0[None, :], 0.0)
    ar1 = jnp.where(keep1, kr[:, :, 1], 0.0)
    ar1 = ar1 + jnp.where((rows == 1)[:, None, None], eye * n1[None, :], 0.0)
    l00, m0 = chol_inv(a00)
    stack0 = jnp.concatenate([a10, ar0.reshape(-1, tile)], axis=0)
    sol0 = mm(stack0, m0)
    l01 = sol0[:tile]
    lr0 = sol0[tile:].reshape(nr, tile, tile)
    lr0 = jnp.where((rows == 0)[:, None, None], l00[None], lr0)
    s11 = a11 - mm(l01, l01)
    upd1 = mm(lr0.reshape(-1, tile), l01).reshape(nr, tile, tile)
    ar1 = ar1 - jnp.where((rows >= 1)[:, None, None], upd1, 0.0)
    l11, m1 = chol_inv(s11)
    lr1 = mm(ar1.reshape(-1, tile), m1).reshape(nr, tile, tile)
    lr1 = jnp.where(
        (rows > 1)[:, None, None], lr1, jnp.where((rows == 1)[:, None, None], l11[None], 0.0)
    )
    kout = kernel_tile(points, xcols.reshape(-1, points.shape[1]), weights)
    kout = kout.reshape(tile, blocks, tile).transpose(1, 0, 2)
    bsr = band_start[my_row]
    keep = ((cols >= bsr) & (cols <= my_row))[:, None, None]
    aout = jnp.where(keep, kout, 0.0)
    aout = aout + jnp.where((cols == my_row)[:, None, None], eye * nugget[None, :], 0.0)
    left = jnp.concatenate([lr0[0], lr1[0]], axis=1)
    right = jnp.concatenate([lr0[1:], lr1[1:]], axis=2).reshape(-1, 2 * tile)
    prod = mm(left, right).reshape(tile, blocks, tile).transpose(1, 0, 2)
    live = ((cols > 1) & (cols <= my_row))[:, None, None]
    res = aout - jnp.where(live, prod, 0.0)
    res = jnp.where((cols == 0)[:, None, None], lr0[0][None], res)
    res = jnp.where((cols == 1)[:, None, None], lr1[0][None], res)
    return res.reshape(1, blocks, 1, tile, tile)


def solution(mesh):
    placed = (P("row", None), P("row"), P(), P())
    return jax.shard_map(
        body,
        mesh=mesh,
        in_specs=placed,
        out_specs=P("row", None, "col", None, None),
        check_vma=False,
    )
```

profile of v0, /device:TPU:8, one launch (start us, length us, event | category | flops | bytes accessed | tf_op | source)
XLA Modules:
  0.0 564.2 jit_solution(12527684723368307736)
XLA Ops:
  6.5 11.4 %all-to-all-start = ((f32[32,16,256]{2,1,0:T(8,128)}), f32[32,16,256]{2,1,0:T(8,128)S(1)}, u32[]{:S(2)}, u32[]{:S(2)}) async-start(f32[32,16,256]{2,1,0:T(8,128)} %bitcast.199), calls=%async_computation | async-start | bytes 1048576 | tf_op jit(solution)/shard_map/all_to_all | solution.py:41
  18.1 16.6 %all-to-all-done = f32[32,16,256]{2,1,0:T(8,128)S(1)} async-done(((f32[32,16,256]{2,1,0:T(8,128)}), f32[32,16,256]{2,1,0:T(8,128)S(1)}, u32[]{:S(2)}, u32[]{:S(2)}) %all-to-all-start) | async-done | bytes 524320 | tf_op jit(solution)/shard_map/all_to_all | solution.py:41
  37.1 48.4 %all-gather = f32[32,1,512]{2,1,0:T(1,128)S(1)} all-gather(f32[1,1,512]{2,1,0:T(1,128)} %bitcast.205), channel_id=1, replica_groups=mesh['row'=32,'col'=8] {'row'}, dimensions={0}, use_global_device_ids=true | all-gather | bytes 67584 | tf_op jit(solution)/shard_map/all_gather | solution.py:47
  90.2 22.2 %all-gather.3.cloned.1.call-done = f32[6,512,256]{2,1,0:T(8,128)} async-done(((f32[6,16,256]{2,1,0:T(8,128)}), f32[6,512,256]{2,1,0:T(8,128)}) %all-gather.3.cloned.1.call-update) | async-done | bytes 3145744 | tf_op jit(solution)/shard_map/all_gather | solution.py:46
  114.0 5.7 %exponential_multiply_fusion.2 = f32[1024,1024]{0,1:T(8,128)S(1)} fusion(f32[1024]{0:T(1024)S(1)} %get-tuple-element.24, f32[1024]{0:T(1024)S(1)} %get-tuple-element.23, f32[256]{0:T(256)S(1)} %copy-done.21, f32[512,256]{1,0:T(8,128)S(1)} %get-tuple-element.58, f32[512,256]{1,0:T(8,128)S(1)} %get-tuple-element.57), kind=kOutput, calls=%fused_computation.34 | convolution fusion | flops 3230400512 | bytes 5252096 | tf_op jit(solution)/shard_map/dot_general | solution.py:10
  123.9 11.9 %cholesky.286 = f32[128,128]{1,0:T(8,128)S(1)} custom-call(f32[128,128]{1,0:T(8,128)S(1)} %cholesky.426), custom_call_target="Cholesky" | custom-call | tf_op jit(solution)/shard_map/jit(cholesky)/cholesky | solution.py:26
  136.0 9.8 %custom-call.27 = f32[1,128,128]{1,2,0:T(8,128)S(1)} custom-call(f32[1,128,128]{2,1,0:T(8,128)S(1)} %get-tuple-element.84), custom_call_target="InvertDiagBlocksLowerTriangular" | custom-call | tf_op jit(solution)/shard_map/jit(cholesky)/cholesky | solution.py:26
  148.3 11.7 %cholesky.305 = f32[128,128]{1,0:T(8,128)S(1)} custom-call(f32[128,128]{1,0:T(8,128)S(1)} %cholesky.430), custom_call_target="Cholesky" | custom-call | tf_op jit(solution)/shard_map/jit(cholesky)/cholesky | solution.py:26
  160.1 9.8 %custom-call.28 = f32[1,128,128]{1,2,0:T(8,128)S(1)} custom-call(f32[1,128,128]{2,1,0:T(8,128)S(1)} %get-tuple-element.81), custom_call_target="InvertDiagBlocksLowerTriangular" | custom-call | tf_op jit(solution)/shard_map/jit(cholesky)/cholesky | solution.py:26
  171.5 11.9 %cholesky.326 = f32[128,128]{1,0:T(8,128)S(1)} custom-call(f32[128,128]{1,0:T(8,128)S(1)} %cholesky.435), custom_call_target="Cholesky" | custom-call | tf_op jit(solution)/shard_map/jit(cholesky)/cholesky | solution.py:26
  184.1 9.8 %custom-call.29 = f32[1,128,128]{1,2,0:T(8,128)S(1)} custom-call(f32[1,128,128]{2,1,0:T(8,128)S(1)} %get-tuple-element.78), custom_call_target="InvertDiagBlocksLowerTriangular" | custom-call | tf_op jit(solution)/shard_map/jit(cholesky)/cholesky | solution.py:26
  195.3 11.7 %cholesky.343 = f32[128,128]{1,0:T(8,128)S(1)} custom-call(f32[128,128]{1,0:T(8,128)S(1)} %convolution_subtract_fusion.12), custom_call_target="Cholesky" | custom-call | tf_op jit(solution)/shard_map/jit(cholesky)/cholesky | solution.py:26
  212.1 12.3 %while.4 = (s32[]{:T(128)}, f32[512,512]{1,0:T(8,128)}, s32[4,2]{0,1:T(2,128)S(1)}, f32[4,128,128]{2,1,0:T(8,128)S(1)}, s32[]{:T(128)}) while((s32[]{:T(128)}, f32[512,512]{1,0:T(8,128)}, s32[4,2]{0,1:T(2,128)S(1)}, f32[4,128,128]{2,1,0:T(8,128)S(1)}, s32[]{:T(128)}) %tuple.69), condition=%wide.while_cond, body=%wide.while_body.sunk | while | flops 2 | bytes 131181 | solution.py:28
  213.2 2.3 bitcast_dynamic-update-slice_fusion.4
  216.2 2.3 bitcast_dynamic-update-slice_fusion.4
  219.2 2.3 bitcast_dynamic-update-slice_fusion.4
  222.2 2.2 bitcast_dynamic-update-slice_fusion.4
  224.5 39.3 %custom-call.30 = f32[4,128,128]{1,2,0:T(8,128)S(1)} custom-call(f32[4,128,128]{2,1,0:T(8,128)S(1)} %get-tuple-element.21), custom_call_target="InvertDiagBlocksLowerTriangular" | custom-call | tf_op jit(solution)/shard_map/jit(_solve_triangular)/triangular_solve | solution.py:28
  268.4 2.4 convolution_subtract_fusion.6
  272.8 2.6 copy.47
  279.6 17.7 %exponential_multiply_fusion = f32[2560,1024]{1,0:T(8,128)} fusion(f32[2560,256]{1,0:T(8,128)} %bitcast_multiply_fusion, f32[1024]{0:T(1024)S(1)} %get-tuple-element.24, f32[2560]{0:T(1024)S(1)} %add.168, f32[512,256]{1,0:T(8,128)} %copy-done.15, f32[512,256]{1,0:T(8,128)S(1)} %copy-done.14), kind=kOutput, calls=%fused_computation.5 | convolution fusion | flops 8074297344 | bytes 14170112 | tf_op jit(solution)/shard_map/dot_general | solution.py:10
  297.4 14.3 %reshape.264 = f32[5,512,2,512]{3,2,1,0:T(2,128)} reshape(f32[2560,1024]{1,0:T(8,128)} %exponential_multiply_fusion) | data formatting | bytes 20971520 | tf_op jit(solution)/shard_map/reshape | solution.py:61
  311.7 13.6 %fusion.133 = (f32[5,512,1,512]{3,2,1,0:T(1,128)}, f32[5,512,1,512]{3,2,1,0:T(1,128)S(1)}) fusion(f32[5,512,2,512]{3,2,1,0:T(2,128)} %reshape.264), kind=kLoop, calls=%fused_computation.240 | loop fusion | bytes 20971520 | tf_op jit(solution)/shard_map/slice | solution.py:67
  325.3 3.2 copy.70
  328.4 2.6 copy.48
  331.0 3.6 fusion.13
  334.7 11.8 %fusion.4 = f32[3072,512]{1,0:T(8,128)S(1)} fusion(f32[2560,512]{1,0:T(8,128)S(1)} %fusion.13, f32[512,512]{1,0:T(8,128)S(1)} %copy-done.9, f32[128,512]{1,0:T(8,128)S(1)} %copy-done.16, f32[128,512]{1,0:T(8,128)S(1)} %fusion.108, f32[128,512]{1,0:T(8,128)S(1)} %fusion.110, f32[128,512]{1,0:T(8,128)S(1)} %fusion.85), kind=kOutput, calls=%fused_computation.10 | convolution fusion | flops 9666035712 | bytes 13631488 | tf_op jit(solution)/shard_map/dot_general | solution.py:10
  346.5 2.6 copy-done.1
  349.1 3.1 convolution_subtract_fusion
  356.0 11.7 %cholesky.358 = f32[128,128]{1,0:T(8,128)S(1)} custom-call(f32[128,128]{1,0:T(8,128)S(1)} %cholesky.439), custom_call_target="Cholesky" | custom-call | tf_op jit(solution)/shard_map/jit(cholesky)/cholesky | solution.py:26
  367.8 9.8 %custom-call.31 = f32[1,128,128]{1,2,0:T(8,128)S(1)} custom-call(f32[1,128,128]{2,1,0:T(8,128)S(1)} %get-tuple-element.72), custom_call_target="InvertDiagBlocksLowerTriangular" | custom-call | tf_op jit(solution)/shard_map/jit(cholesky)/cholesky | solution.py:26
  380.2 11.9 %cholesky.377 = f32[128,128]{1,0:T(8,128)S(1)} custom-call(f32[128,128]{1,0:T(8,128)S(1)} %cholesky.443), custom_call_target="Cholesky" | custom-call | tf_op jit(solution)/shard_map/jit(cholesky)/cholesky | solution.py:26
  393.4 9.8 %custom-call.32 = f32[1,128,128]{1,2,0:T(8,128)S(1)} custom-call(f32[1,128,128]{2,1,0:T(8,128)S(1)} %get-tuple-element.69), custom_call_target="InvertDiagBlocksLowerTriangular" | custom-call | tf_op jit(solution)/shard_map/jit(cholesky)/cholesky | solution.py:26
  404.8 11.7 %cholesky.398 = f32[128,128]{1,0:T(8,128)S(1)} custom-call(f32[128,128]{1,0:T(8,128)S(1)} %cholesky.448), custom_call_target="Cholesky" | custom-call | tf_op jit(solution)/shard_map/jit(cholesky)/cholesky | solution.py:26
  417.2 9.8 %custom-call.33 = f32[1,128,128]{1,2,0:T(8,128)S(1)} custom-call(f32[1,128,128]{2,1,0:T(8,128)S(1)} %get-tuple-element.66), custom_call_target="InvertDiagBlocksLowerTriangular" | custom-call | tf_op jit(solution)/shard_map/jit(cholesky)/cholesky | solution.py:26
  428.4 12.1 %cholesky.415 = f32[128,128]{1,0:T(8,128)S(1)} custom-call(f32[128,128]{1,0:T(8,128)S(1)} %convolution_subtract_fusion.11), custom_call_target="Cholesky" | custom-call | tf_op jit(solution)/shard_map/jit(cholesky)/cholesky | solution.py:26
  445.2 11.6 %while.5 = (s32[]{:T(128)}, f32[512,512]{1,0:T(8,128)}, s32[4,2]{0,1:T(2,128)S(1)}, f32[4,128,128]{2,1,0:T(8,128)S(1)}, s32[]{:T(128)}) while((s32[]{:T(128)}, f32[512,512]{1,0:T(8,128)}, s32[4,2]{0,1:T(2,128)S(1)}, f32[4,128,128]{2,1,0:T(8,128)S(1)}, s32[]{:T(128)}) %tuple.77), condition=%wide.while_cond.clone, body=%wide.while_body.clone.sunk | while | flops 2 | bytes 131181 | solution.py:28
  448.8 2.2 bitcast_dynamic-update-slice_fusion.5
  451.7 2.2 bitcast_dynamic-update-slice_fusion.5
  456.8 39.3 %custom-call.34 = f32[4,128,128]{1,2,0:T(8,128)S(1)} custom-call(f32[4,128,128]{2,1,0:T(8,128)S(1)} %get-tuple-element.22), custom_call_target="InvertDiagBlocksLowerTriangular" | custom-call | tf_op jit(solution)/shard_map/jit(_solve_triangular)/triangular_solve | solution.py:28
  500.8 2.6 convolution_subtract_fusion.5
  503.8 3.6 bitcast_select_fusion.2
  507.5 10.8 %fusion.48 = f32[5,512,512]{2,1,0:T(8,128)S(1)} fusion(f32[5,512,512]{2,1,0:T(8,128)S(1)} %bitcast.195, f32[3072,512]{1,0:T(8,128)} %copy-done.1), kind=kOutput, calls=%fused_computation.90 | convolution fusion | flops 8053063680 | bytes 11534336 | tf_op jit(solution)/shard_map/dot_general | solution.py:10
  518.3 9.8 %select_select_fusion = f32[5,512,512]{2,1,0:T(8,128)S(1)} fusion(f32[5,512,1,512]{3,2,1,0:T(1,128)S(1)} %bitcast.198, f32[5,512,512]{2,1,0:T(8,128)S(1)} %fusion.48, f32[512,512]{1,0:T(8,128)S(1)} %copy-done.19, f32[512,512]{1,0:T(8,128)S(1)} %copy-done.18, pred[5]{0:T(512)(128)(4,1)S(1)} %get-tuple-element.89, pred[5]{0:T(512)(128)(4,1)S(1)} %get-tuple-element.88, ...), kind=kOutput, calls=%fused_computation.23 | convolution fusion | flops 8063025152 | bytes 18874388 | tf_op jit(solution)/shard_map/dot_general | solution.py:10
  528.1 2.3 copy-done.5
  531.9 2.6 copy-done.2
  535.4 5.8 %exponential_multiply_fusion.1 = f32[512,2048]{1,0:T(8,128)S(1)} fusion(f32[2048,256]{1,0:T(8,128)S(1)} %bitcast.196, f32[2048]{0:T(1024)S(1)} %bitcast.207, f32[512]{0:T(512)S(1)} %fusion.72, f32[512,256]{1,0:T(8,128)S(1)} %copy-done.8, f32[256]{0:T(256)S(1)} %copy-done.21), kind=kOutput, calls=%fused_computation.33 | convolution fusion | flops 3229745152 | bytes 6827008 | tf_op jit(solution)/shard_map/dot_general | solution.py:10
  541.3 15.7 %fusion.21 = f32[1,4,1,512,512]{4,3,2,1,0:T(8,128)} fusion(f32[64,4,8,512]{3,2,1,0:T(8,128)S(1)} %bitcast.208, f32[512,512]{1,0:T(8,128)S(1)} %copy-done.17, f32[512,512]{1,0:T(8,128)S(1)} %slice_bitcast_fusion, f32[512,512]{1,0:T(8,128)S(1)} %slice_bitcast_fusion.1, pred[4]{0:T(512)(128)(4,1)S(1)} %get-tuple-element.95, ...), kind=kOutput, calls=%fused_computation.32 | convolution fusion | flops 12894863360 | bytes 19922964 | tf_op jit(solution)/shard_map/dot_general | solution.py:10
  (165 shorter events, 63.2 us)
Async XLA Ops:
  6.5 80.5 %copy-start = (s32[32]{0:T(128)S(1)}, s32[32]{0:T(128)}, u32[]{:S(2)}) copy-start(s32[32]{0:T(128)} %param.10) | copy-start | bytes 388
  6.5 81.1 %copy-start.22 = (f32[512]{0:T(512)S(1)}, f32[512]{0:T(512)}, u32[]{:S(2)}) copy-start(f32[512]{0:T(512)} %param.8) | copy-start | bytes 6148
  6.5 83.3 %copy-start.6 = (f32[512,256]{1,0:T(8,128)S(1)}, f32[512,256]{1,0:T(8,128)}, u32[]{:S(2)}) copy-start(f32[512,256]{1,0:T(8,128)} %param.7) | copy-start | bytes 1572868
  6.5 83.4 %copy-start.21 = (f32[256]{0:T(256)S(1)}, f32[256]{0:T(256)}, u32[]{:S(2)}) copy-start(f32[256]{0:T(256)} %param.9) | copy-start | bytes 3076
  6.5 28.2 %all-to-all-start = ((f32[32,16,256]{2,1,0:T(8,128)}), f32[32,16,256]{2,1,0:T(8,128)S(1)}, u32[]{:S(2)}, u32[]{:S(2)}) async-start(f32[32,16,256]{2,1,0:T(8,128)} %bitcast.199), calls=%async_computation | async-start | bytes 1048576 | tf_op jit(solution)/shard_map/all_to_all | solution.py:41
  18.0 94.4 %all-gather.3.cloned.1.call-start = ((), (), s32[]{:S(2)}) async-start(), calls=%async_computation.1 | async-start | bytes 3244032 | tf_op jit(solution)/shard_map/all_gather | solution.py:46
  113.6 6.1 %copy-start.13 = (f32[512,256]{1,0:T(8,128)}, f32[512,256]{1,0:T(8,128)S(1)}, u32[]{:S(2)}) copy-start(f32[512,256]{1,0:T(8,128)S(1)} %get-tuple-element.57) | copy-start | bytes 1572868
  113.6 6.1 %copy-start.15 = (f32[512,256]{1,0:T(8,128)}, f32[512,256]{1,0:T(8,128)S(1)}, u32[]{:S(2)}) copy-start(f32[512,256]{1,0:T(8,128)S(1)} %get-tuple-element.58) | copy-start | bytes 1572868
  119.7 2.6 copy-start.12
  122.9 1.0 copy-start.11
  263.8 4.2 copy-start.20
  268.4 9.0 %copy-start.7 = (f32[512,256]{1,0:T(8,128)S(1)}, f32[512,256]{1,0:T(8,128)}, u32[]{:S(2)}) copy-start(f32[512,256]{1,0:T(8,128)} %param.7) | copy-start | bytes 1572868
  277.4 2.2 copy-start.3
  277.9 1.7 copy-start.14
  331.0 3.7 copy-start.9
  331.0 3.7 copy-start.16
  346.4 2.6 copy-start.1
  355.0 1.0 copy-start.10
  500.8 17.5 %slice-start.1 = ((s8[5242880]{0:T(1024)(128)(4,1)}), s8[4194304]{0:T(1024)(128)(4,1)S(1)}, s32[]{:S(2)}) async-start(s8[5242880]{0:T(1024)(128)(4,1)} %bitcast.197), calls=%async_computation.3 | async-start | bytes 8388608
  503.8 14.5 %slice-start.2 = ((s8[5242880]{0:T(1024)(128)(4,1)}), s8[1048576]{0:T(1024)(128)(4,1)S(1)}, s32[]{:S(2)}) async-start(s8[5242880]{0:T(1024)(128)(4,1)} %bitcast.197), calls=%async_computation.4 | async-start | bytes 2097152
  507.4 10.8 %copy-start.18 = (f32[512,512]{1,0:T(8,128)S(1)}, f32[512,512]{1,0:T(8,128)}, u32[]{:S(2)}) copy-start(f32[512,512]{1,0:T(8,128)} %copy.44) | copy-start | bytes 3145732
  507.4 10.8 %copy-start.19 = (f32[512,512]{1,0:T(8,128)S(1)}, f32[512,512]{1,0:T(8,128)}, u32[]{:S(2)}) copy-start(f32[512,512]{1,0:T(8,128)} %get-tuple-element.42) | copy-start | bytes 3145732
  528.1 2.3 copy-start.5
  531.8 2.7 copy-start.2
  531.9 3.2 copy-start.4
  531.9 3.6 copy-start.8
  535.4 5.8 %slice-start = ((f32[5,512,512]{2,1,0:T(8,128)}), f32[4,512,512]{2,1,0:T(8,128)S(1)}, s32[]{:S(2)}) async-start(f32[5,512,512]{2,1,0:T(8,128)} %copy-done.2), calls=%async_computation.2 | async-start | bytes 8388608 | tf_op jit(solution)/shard_map/slice | solution.py:90
  535.4 5.8 %slice-start.3 = ((f32[5,512,512]{2,1,0:T(8,128)}), f32[4,512,512]{2,1,0:T(8,128)S(1)}, s32[]{:S(2)}) async-start(f32[5,512,512]{2,1,0:T(8,128)} %copy-done.5), calls=%async_computation.5 | async-start | bytes 8388608 | tf_op jit(solution)/shard_map/slice | solution.py:90
  535.4 5.8 %copy-start.17 = (f32[512,512]{1,0:T(8,128)S(1)}, f32[512,512]{1,0:T(8,128)}, u32[]{:S(2)}) copy-start(f32[512,512]{1,0:T(8,128)} %copy.59) | copy-start | bytes 3145732
Sparse Core Ops, SparseCore 0:
  35.5 76.7 all-gather.2
where the time goes:
time: 575 us; the launch traced here: 564 us
  other arithmetic  258 us (45%)
  matrix products  108 us (19%)
  local copies, waits for them, and re-layouts  78.9 us (14%)
  blocking collectives  48.4 us (8%)
  waiting for transfers between devices  38.8 us (7%)
  between operations  19.7 us (3%)
  starting transfers between devices  11.5 us (2%)
    another operation x29, other arithmetic, chol_inv(): low = jnp.linalg.cholesky(a)  158 us
    another operation x5, other arithmetic, chol_inv(): inv = jax.scipy.linalg.solve_triangular(low, eye, lower=True)  81.5 us
    dot_general x8, matrix products, mm(): lax.dot_general(a, b, (((1,), (1,)), ((), ())), precision=HI, preferred_e...  80.4 us
    all_gather x1, blocking collectives, body(): nug = lax.all_gather(nugget, 'row', tiled=True)  48.4 us
    another operation x27, local copies, waits for them, and re-layouts, chol_inv(): inv = jax.scipy.linalg.solve_triangular(low, eye, lower=True)  23.4 us
    all_gather x1, waiting for transfers between devices, body(): tiles_x = lax.all_gather(sel, 'row', axis=1, tiled=True)  22.2 us
    all_to_all x1, waiting for transfers between devices, body(): recv = lax.all_to_all(chunks, 'row', 0, 0, tiled=True)  16.6 us
    another operation x14, matrix products, chol_inv(): inv = jax.scipy.linalg.solve_triangular(low, eye, lower=True)  16.6 us
  transfers between devices with their start and end apart: 2, of which 2 were waited for; matrix products, arithmetic and copies ran while one was open for 1% of the time, Pallas kernels for 0%

commit v1 on v0

--- a/solution.py
+++ b/solution.py
@@ -44,7 +44,9 @@
     )[:, 0]
     sel = jnp.concatenate([recv[:2], mine], axis=0)
     tiles_x = lax.all_gather(sel, "row", axis=1, tiled=True)
-    nug = lax.all_gather(nugget, "row", tiled=True)
+    o_now = lax.axis_size("row")
+    left_arr = jnp.concatenate(o_now * [nugget], axis=0)
+    nug = lax.all_to_all(left_arr, "row", 0, 0, tiled=True)
     x0, x1 = (tiles_x[0], tiles_x[1])
     xcols = tiles_x[2:]
     n0, n1 = (nug[:tile], nug[tile : 2 * tile])

time: 575 us -> 628 us (1.092)
  blocking collectives: 48.4 us -> 0 us
  waiting for transfers between devices: 38.8 us -> 79 us
  local copies, waits for them, and re-layouts: 78.9 us -> 105 us
  other arithmetic: 258 us -> 276 us
  matrix products: 108 us -> 119 us
    all_gather x1 -> x0, blocking collectives: 48.4 us -> none  [body(): nug = lax.all_gather(nugget, 'row', tiled=True)]
    all_gather x1, waiting for transfers between devices: 22.2 us -> 58.5 us  [body(): tiles_x = lax.all_gather(sel, 'row', axis=1, tiled=True)]
    another operation x29, other arithmetic: 158 us -> 169 us  [chol_inv(): low = jnp.linalg.cholesky(a)]
    unnamed x52 -> x57, local copies, waits for them, and re-layouts: 14.4 us -> 25 us
    dot_general x8, matrix products: 80.4 us -> 87.9 us  [mm(): lax.dot_general(a, b, (((1,), (1,)), ((), ())), precision=HI, preferred_e...]
  transfers between devices with their start and end apart: 2 -> 3, of which waited for: 2 -> 3; matrix products, arithmetic and copies ran while one was open for 1% -> 1% of each run, Pallas kernels for 0% -> 0%
where the time goes in v1:
time: 628 us; the launch traced here: 616 us
  other arithmetic  276 us (44%)
  matrix products  119 us (19%)
  local copies, waits for them, and re-layouts  105 us (17%)
  waiting for transfers between devices  79 us (13%)
  between operations  19.7 us (3%)
  starting transfers between devices  17.3 us (3%)
    another operation x29, other arithmetic, chol_inv(): low = jnp.linalg.cholesky(a)  169 us
    dot_general x8, matrix products, mm(): lax.dot_general(a, b, (((1,), (1,)), ((), ())), precision=HI, preferred_e...  87.9 us
    another operation x5, other arithmetic, chol_inv(): inv = jax.scipy.linalg.solve_triangular(low, eye, lower=True)  82.1 us
    all_gather x1, waiting for transfers between devices, body(): tiles_x = lax.all_gather(sel, 'row', axis=1, tiled=True)  58.5 us
    unnamed x57, local copies, waits for them, and re-layouts  25 us
    another operation x27, local copies, waits for them, and re-layouts, chol_inv(): inv = jax.scipy.linalg.solve_triangular(low, eye, lower=True)  23 us
    another operation x14, matrix products, chol_inv(): inv = jax.scipy.linalg.solve_triangular(low, eye, lower=True)  20.6 us
    all_to_all x1, waiting for transfers between devices, body(): recv = lax.all_to_all(chunks, 'row', 0, 0, tiled=True)  16.7 us
  transfers between devices with their start and end apart: 3, of which 3 were waited for; matrix products, arithmetic and copies ran while one was open for 1% of the time, Pallas kernels for 0%

profile of v1, /device:TPU:8, one launch (start us, length us, event | category | flops | bytes accessed | tf_op | source)
XLA Modules:
  0.0 616.0 jit_solution(777780185831607041)
XLA Ops:
  6.5 11.4 %all-to-all-start = ((f32[32,16,256]{2,1,0:T(8,128)}), f32[32,16,256]{2,1,0:T(8,128)S(1)}, u32[]{:S(2)}, u32[]{:S(2)}) async-start(f32[32,16,256]{2,1,0:T(8,128)} %bitcast.194), calls=%async_computation | async-start | bytes 1048576 | tf_op jit(solution)/shard_map/all_to_all | solution.py:41
  18.0 16.7 %all-to-all-done = f32[32,16,256]{2,1,0:T(8,128)S(1)} async-done(((f32[32,16,256]{2,1,0:T(8,128)}), f32[32,16,256]{2,1,0:T(8,128)S(1)}, u32[]{:S(2)}, u32[]{:S(2)}) %all-to-all-start) | async-done | bytes 524320 | tf_op jit(solution)/shard_map/all_to_all | solution.py:41
  36.7 5.8 all-to-all-start.1
  48.7 3.9 all-to-all-done.1
  53.8 58.5 %all-gather.2.cloned.1.call-done = f32[6,512,256]{2,1,0:T(8,128)} async-done(((f32[6,16,256]{2,1,0:T(8,128)}), f32[6,512,256]{2,1,0:T(8,128)}) %all-gather.2.cloned.1.call-update) | async-done | bytes 3145744 | tf_op jit(solution)/shard_map/all_gather | solution.py:46
  114.0 5.7 exponential_multiply_fusion.2
  123.9 11.7 %cholesky.286 = f32[128,128]{1,0:T(8,128)S(1)} custom-call(f32[128,128]{1,0:T(8,128)S(1)} %cholesky.426), custom_call_target="Cholesky" | custom-call | tf_op jit(solution)/shard_map/jit(cholesky)/cholesky | solution.py:26
  135.8 10.0 %custom-call.27 = f32[1,128,128]{1,2,0:T(8,128)S(1)} custom-call(f32[1,128,128]{2,1,0:T(8,128)S(1)} %get-tuple-element.84), custom_call_target="InvertDiagBlocksLowerTriangular" | custom-call | tf_op jit(solution)/shard_map/jit(cholesky)/cholesky | solution.py:26
  148.3 11.7 %cholesky.305 = f32[128,128]{1,0:T(8,128)S(1)} custom-call(f32[128,128]{1,0:T(8,128)S(1)} %cholesky.430), custom_call_target="Cholesky" | custom-call | tf_op jit(solution)/shard_map/jit(cholesky)/cholesky | solution.py:26
  160.0 9.8 %custom-call.28 = f32[1,128,128]{1,2,0:T(8,128)S(1)} custom-call(f32[1,128,128]{2,1,0:T(8,128)S(1)} %get-tuple-element.81), custom_call_target="InvertDiagBlocksLowerTriangular" | custom-call | tf_op jit(solution)/shard_map/jit(cholesky)/cholesky | solution.py:26
  171.4 22.5 %cholesky.326 = f32[128,128]{1,0:T(8,128)S(1)} custom-call(f32[128,128]{1,0:T(8,128)S(1)} %cholesky.435), custom_call_target="Cholesky" | custom-call | tf_op jit(solution)/shard_map/jit(cholesky)/cholesky | solution.py:26
  194.7 9.8 %custom-call.29 = f32[1,128,128]{1,2,0:T(8,128)S(1)} custom-call(f32[1,128,128]{2,1,0:T(8,128)S(1)} %get-tuple-element.78), custom_call_target="InvertDiagBlocksLowerTriangular" | custom-call | tf_op jit(solution)/shard_map/jit(cholesky)/cholesky | solution.py:26
  206.0 11.7 %cholesky.343 = f32[128,128]{1,0:T(8,128)S(1)} custom-call(f32[128,128]{1,0:T(8,128)S(1)} %convolution_subtract_fusion.12), custom_call_target="Cholesky" | custom-call | tf_op jit(solution)/shard_map/jit(cholesky)/cholesky | solution.py:26
  222.9 12.0 %while.4 = (s32[]{:T(128)}, f32[512,512]{1,0:T(8,128)}, s32[4,2]{0,1:T(2,128)S(1)}, f32[4,128,128]{2,1,0:T(8,128)S(1)}, s32[]{:T(128)}) while((s32[]{:T(128)}, f32[512,512]{1,0:T(8,128)}, s32[4,2]{0,1:T(2,128)S(1)}, f32[4,128,128]{2,1,0:T(8,128)S(1)}, s32[]{:T(128)}) %tuple.69), condition=%wide.while_cond, body=%wide.while_body.sunk | while | flops 2 | bytes 131181 | solution.py:28
  223.6 2.3 bitcast_dynamic-update-slice_fusion.4
  226.6 2.3 bitcast_dynamic-update-slice_fusion.4
  234.8 39.3 %custom-call.30 = f32[4,128,128]{1,2,0:T(8,128)S(1)} custom-call(f32[4,128,128]{2,1,0:T(8,128)S(1)} %get-tuple-element.21), custom_call_target="InvertDiagBlocksLowerTriangular" | custom-call | tf_op jit(solution)/shard_map/jit(_solve_triangular)/triangular_solve | solution.py:28
  278.8 2.4 convolution_subtract_fusion.6
  283.2 2.5 copy.29
  290.0 18.0 %exponential_multiply_fusion = f32[2560,1024]{1,0:T(8,128)} fusion(f32[2560,256]{1,0:T(8,128)} %bitcast_multiply_fusion, f32[1024]{0:T(1024)S(1)} %get-tuple-element.24, f32[2560]{0:T(1024)S(1)} %add.168, f32[512,256]{1,0:T(8,128)} %copy-done.19, f32[512,256]{1,0:T(8,128)S(1)} %copy-done.18), kind=kOutput, calls=%fused_computation.5 | convolution fusion | flops 8074297344 | bytes 14170112 | tf_op jit(solution)/shard_map/dot_general | solution.py:10
  308.0 14.3 %reshape.304 = f32[5,512,2,512]{3,2,1,0:T(2,128)} reshape(f32[2560,1024]{1,0:T(8,128)} %exponential_multiply_fusion) | data formatting | bytes 20971520 | tf_op jit(solution)/shard_map/reshape | solution.py:63
  322.3 13.5 %fusion.132 = (f32[5,512,1,512]{3,2,1,0:T(1,128)}, f32[5,512,1,512]{3,2,1,0:T(1,128)S(1)}) fusion(f32[5,512,2,512]{3,2,1,0:T(2,128)} %reshape.304), kind=kLoop, calls=%fused_computation.239 | loop fusion | bytes 20971520 | tf_op jit(solution)/shard_map/slice | solution.py:69
  335.8 3.2 copy.49
  339.0 2.6 copy.30
  341.6 3.6 fusion.8
  345.2 11.6 %fusion.4 = f32[3072,512]{1,0:T(8,128)S(1)} fusion(f32[2560,512]{1,0:T(8,128)S(1)} %fusion.8, f32[512,512]{1,0:T(8,128)S(1)} %copy-done.8, f32[128,512]{1,0:T(8,128)S(1)} %copy-done.20, f32[128,512]{1,0:T(8,128)S(1)} %fusion.107, f32[128,512]{1,0:T(8,128)S(1)} %fusion.109, f32[128,512]{1,0:T(8,128)S(1)} %fusion.84), kind=kOutput, calls=%fused_computation.10 | convolution fusion | flops 9666035712 | bytes 13631488 | tf_op jit(solution)/shard_map/dot_general | solution.py:10
  356.8 2.6 copy-done
  359.5 3.1 convolution_subtract_fusion
  366.3 11.7 %cholesky.358 = f32[128,128]{1,0:T(8,128)S(1)} custom-call(f32[128,128]{1,0:T(8,128)S(1)} %cholesky.439), custom_call_target="Cholesky" | custom-call | tf_op jit(solution)/shard_map/jit(cholesky)/cholesky | solution.py:26
  378.2 9.8 %custom-call.31 = f32[1,128,128]{1,2,0:T(8,128)S(1)} custom-call(f32[1,128,128]{2,1,0:T(8,128)S(1)} %get-tuple-element.72), custom_call_target="InvertDiagBlocksLowerTriangular" | custom-call | tf_op jit(solution)/shard_map/jit(cholesky)/cholesky | solution.py:26
  390.6 12.1 %cholesky.377 = f32[128,128]{1,0:T(8,128)S(1)} custom-call(f32[128,128]{1,0:T(8,128)S(1)} %cholesky.443), custom_call_target="Cholesky" | custom-call | tf_op jit(solution)/shard_map/jit(cholesky)/cholesky | solution.py:26
  404.0 9.8 %custom-call.32 = f32[1,128,128]{1,2,0:T(8,128)S(1)} custom-call(f32[1,128,128]{2,1,0:T(8,128)S(1)} %get-tuple-element.69), custom_call_target="InvertDiagBlocksLowerTriangular" | custom-call | tf_op jit(solution)/shard_map/jit(cholesky)/cholesky | solution.py:26
  415.3 11.7 %cholesky.398 = f32[128,128]{1,0:T(8,128)S(1)} custom-call(f32[128,128]{1,0:T(8,128)S(1)} %cholesky.448), custom_call_target="Cholesky" | custom-call | tf_op jit(solution)/shard_map/jit(cholesky)/cholesky | solution.py:26
  427.8 9.8 %custom-call.33 = f32[1,128,128]{1,2,0:T(8,128)S(1)} custom-call(f32[1,128,128]{2,1,0:T(8,128)S(1)} %get-tuple-element.66), custom_call_target="InvertDiagBlocksLowerTriangular" | custom-call | tf_op jit(solution)/shard_map/jit(cholesky)/cholesky | solution.py:26
  439.1 11.9 %cholesky.415 = f32[128,128]{1,0:T(8,128)S(1)} custom-call(f32[128,128]{1,0:T(8,128)S(1)} %convolution_subtract_fusion.11), custom_call_target="Cholesky" | custom-call | tf_op jit(solution)/shard_map/jit(cholesky)/cholesky | solution.py:26
  455.7 11.2 %while.5 = (s32[]{:T(128)}, f32[512,512]{1,0:T(8,128)}, s32[4,2]{0,1:T(2,128)S(1)}, f32[4,128,128]{2,1,0:T(8,128)S(1)}, s32[]{:T(128)}) while((s32[]{:T(128)}, f32[512,512]{1,0:T(8,128)}, s32[4,2]{0,1:T(2,128)S(1)}, f32[4,128,128]{2,1,0:T(8,128)S(1)}, s32[]{:T(128)}) %tuple.77), condition=%wide.while_cond.clone, body=%wide.while_body.clone.sunk | while | flops 2 | bytes 131181 | solution.py:28
  466.8 39.9 %custom-call.34 = f32[4,128,128]{1,2,0:T(8,128)} custom-call(f32[4,128,128]{2,1,0:T(8,128)S(1)} %get-tuple-element.22), custom_call_target="InvertDiagBlocksLowerTriangular" | custom-call | tf_op jit(solution)/shard_map/jit(_solve_triangular)/triangular_solve | solution.py:28
  514.1 2.5 convolution_subtract_fusion.5
  519.8 5.7 bitcast_select_fusion.2
  525.5 12.3 %fusion.47 = f32[5,512,512]{1,2,0:T(8,128)} fusion(f32[5,512,512]{2,1,0:T(8,128)S(1)} %bitcast.192, f32[3072,512]{1,0:T(8,128)} %copy-done), kind=kOutput, calls=%fused_computation.89 | convolution fusion | flops 8053063680 | bytes 11534336 | tf_op jit(solution)/shard_map/dot_general | solution.py:10
  537.8 11.8 %copy.50 = f32[5,512,1,512]{1,3,0,2:T(8,128)} copy(f32[5,512,1,512]{3,2,1,0:T(1,128)} %get-tuple-element.51) | data formatting | bytes 10485760
  549.7 13.7 %select_select_fusion = f32[5,512,512]{1,2,0:T(8,128)S(1)} fusion(f32[5,512,1,512]{1,3,0,2:T(8,128)} %copy.50, f32[5,512,512]{1,2,0:T(8,128)} %fusion.47, f32[512,512]{0,1:T(8,128)} %copy.34, f32[512,512]{0,1:T(8,128)S(1)} %copy-done.21, pred[5]{0:T(512)(128)(4,1)S(1)} %get-tuple-element.89, pred[5]{0:T(512)(128)(4,1)S(1)} %get-tuple-element.88, ...), kind=kOutput, calls=%fused_computation.22 | convolution fusion | flops 8063025152 | bytes 18874388 | tf_op jit(solution)/shard_map/dot_general | solution.py:10
  567.1 6.1 copy.36
  573.2 3.3 broadcast_select_fusion
  579.9 2.7 copy.35
  582.6 2.5 copy.37
  585.2 5.8 exponential_multiply_fusion.1
  591.0 17.6 %fusion.20 = f32[1,4,1,512,512]{4,3,2,1,0:T(8,128)} fusion(f32[64,4,8,512]{3,2,1,0:T(8,128)S(1)} %bitcast.202, f32[512,512]{1,0:T(8,128)} %copy.39, f32[512,512]{1,0:T(8,128)} %copy.37, f32[512,512]{1,0:T(8,128)} %copy.35, pred[4]{0:T(512)(128)(4,1)S(1)} %get-tuple-element.95, pred[4]{0:T(512)(128)(4,1)S(1)} %get-tuple-element.97, ...), kind=kOutput, calls=%fused_computation.31 | convolution fusion | flops 12894863360 | bytes 22020116 | tf_op jit(solution)/shard_map/dot_general | solution.py:10
  (175 shorter events, 84.6 us)
Async XLA Ops:
  6.5 42.0 %copy-start.5 = (f32[512,256]{1,0:T(8,128)S(1)}, f32[512,256]{1,0:T(8,128)}, u32[]{:S(2)}) copy-start(f32[512,256]{1,0:T(8,128)} %param.7) | copy-start | bytes 1572868
  6.5 42.0 %copy-start.26 = (f32[256]{0:T(256)S(1)}, f32[256]{0:T(256)}, u32[]{:S(2)}) copy-start(f32[256]{0:T(256)} %param.9) | copy-start | bytes 3076
  6.5 28.2 %all-to-all-start = ((f32[32,16,256]{2,1,0:T(8,128)}), f32[32,16,256]{2,1,0:T(8,128)S(1)}, u32[]{:S(2)}, u32[]{:S(2)}) async-start(f32[32,16,256]{2,1,0:T(8,128)} %bitcast.194), calls=%async_computation | async-start | bytes 1048576 | tf_op jit(solution)/shard_map/all_to_all | solution.py:41
  18.0 94.3 %all-gather.2.cloned.1.call-start = ((), (), s32[]{:S(2)}) async-start(), calls=%async_computation.2 | async-start | bytes 3244032 | tf_op jit(solution)/shard_map/all_gather | solution.py:46
  36.7 15.9 %all-to-all-start.1 = ((f32[32,512,1]{1,2,0:T(1,128)}), f32[32,512,1]{1,2,0:T(1,128)S(1)}, u32[]{:S(2)}, u32[]{:S(2)}) async-start(f32[32,512,1]{1,2,0:T(1,128)} %concatenate.87), calls=%async_computation.1 | async-start | bytes 131072 | tf_op jit(solution)/shard_map/all_to_all | solution.py:49
  113.6 6.1 copy-start.17
  113.6 6.1 copy-start.19
  119.7 2.6 copy-start.14
  122.9 1.0 copy-start.13
  274.2 4.2 copy-start.24
  278.8 9.0 %copy-start.6 = (f32[512,256]{1,0:T(8,128)S(1)}, f32[512,256]{1,0:T(8,128)}, u32[]{:S(2)}) copy-start(f32[512,256]{1,0:T(8,128)} %param.7) | copy-start | bytes 1572868
  287.8 2.2 copy-start.2
  288.3 1.7 copy-start.18
  341.6 3.7 copy-start.8
  341.6 3.7 copy-start.20
  356.8 2.7 copy-start
  365.4 1.0 copy-start.12
  455.6 62.9 %copy-start.9 = (f32[512,512]{1,0:T(8,128)S(1)}, f32[512,512]{1,0:T(8,128)}, u32[]{:S(2)}) copy-start(f32[512,512]{1,0:T(8,128)} %get-tuple-element.42) | copy-start | bytes 3145732
  510.8 5.8 copy-start.15
  514.1 4.5 copy-start.22
  537.8 11.8 %copy-start.16 = (f32[128,512]{1,0:T(8,128)S(1)}, f32[128,512]{1,0:T(8,128)}, u32[]{:S(2)}) copy-start(f32[128,512]{1,0:T(8,128)} %copy-done.15) | copy-start | bytes 786436
  537.8 11.8 %copy-start.21 = (f32[512,512]{0,1:T(8,128)S(1)}, f32[512,512]{0,1:T(8,128)}, u32[]{:S(2)}) copy-start(f32[512,512]{0,1:T(8,128)} %fusion.55) | copy-start | bytes 3145732
  537.8 11.8 %copy-start.23 = (f32[128,512]{1,0:T(8,128)S(1)}, f32[128,512]{1,0:T(8,128)}, u32[]{:S(2)}) copy-start(f32[128,512]{1,0:T(8,128)} %copy-done.22) | copy-start | bytes 786436
  537.8 11.8 %copy-start.25 = (f32[128,512]{1,0:T(8,128)S(1)}, f32[128,512]{1,0:T(8,128)}, u32[]{:S(2)}) copy-start(f32[128,512]{1,0:T(8,128)} %fusion.100) | copy-start | bytes 786436
  563.4 2.3 copy-start.4
  576.5 2.3 copy-start.1
  578.9 6.2 %copy-start.3 = (f32[4,512,256]{2,1,0:T(8,128)S(1)}, f32[4,512,256]{2,1,0:T(8,128)}, u32[]{:S(2)}) copy-start(f32[4,512,256]{2,1,0:T(8,128)} %copy-done.2) | copy-start | bytes 6291460
  578.9 6.2 %copy-start.7 = (f32[512,256]{1,0:T(8,128)S(1)}, f32[512,256]{1,0:T(8,128)}, u32[]{:S(2)}) copy-start(f32[512,256]{1,0:T(8,128)} %param.7) | copy-start | bytes 1572868
  585.1 5.9 slice-start
  585.1 5.9 slice-start.1
  585.1 5.9 copy-start.10
  585.1 5.9 copy-start.11
Sparse Core Ops, SparseCore 0:
  35.5 76.7 all-gather.1
